TPU v7x, 256 devices: a whole 4x4x8 slice. The times are simulated.
256 devices in a mesh: dp: 8 (over z_lo, x), expert: 32 (over z_hi, y, core).
Axes of the slice: x: 4, y: 4, z: 8 (z_hi: 4, z_lo: 2; z = z_hi * 2 + z_lo), core: 2. Of those that a mesh axis runs over, the one named last changes fastest.
Arguments:
- tokens: bfloat16 [8192, 4096], P('expert', 'dp'), may hold values from -6 to 6
- out_grad: bfloat16 [8192, 4096], P('expert', 'dp'), may hold values from -3 to 3
- expert_ids: int32 [8192, 2], P('expert'), may hold values from 0 to 31, as said below
- gate_probs: float32 [8192, 2], P('expert'), may hold values from 0.25 to 1
- w_gate: bfloat16 [32, 4096, 1024], P('expert', 'dp'), may hold values from -0.09375 to 0.09375
- w_up: bfloat16 [32, 4096, 1024], P('expert', 'dp'), may hold values from -0.09375 to 0.09375
- w_down: bfloat16 [32, 1024, 4096], P('expert', None, 'dp'), may hold values from -0.1875 to 0.1875
Outputs:
- token_grad: bfloat16 [8192, 4096], P('expert', 'dp')
- grad_w_gate: float32 [32, 4096, 1024], P('expert', 'dp')
- grad_w_up: float32 [32, 4096, 1024], P('expert', 'dp')
- grad_w_down: float32 [32, 1024, 4096], P('expert', None, 'dp')
Inputs may be any that keep to these rules, and one draw needn't show every extreme that they name: `expert_ids`: A token's two ids differ. Among the tokens of one aligned block of 256 tokens no expert is named more than 32 times; 4 experts, the same for every block, are named exactly 32 times in each block.
All inputs are finite; a program needn't handle non-finite values.
Results may differ from a plain program's by a relative error of at most 0.02.
Values may be sent and summed in bfloat16 or wider, within the bound.
No kernel may reach another device: no remote copies, remote signals or barrier semaphores. Data moves between devices by JAX's collectives and lax.ppermute only.
A program may use at most 64 MiB of HBM per device.

v0:
```python
import jax
import jax.numpy as jnp
from jax import lax
from jax.sharding import PartitionSpec as P

MOST = 32
contract_rows = (((0,), (0,)), ((), ()))
contract_cols = (((1,), (1,)), ((), ()))


def silu_parts(pre_gate):
    sigmoid_gate = jax.nn.sigmoid(pre_gate)
    return (pre_gate * sigmoid_gate, sigmoid_gate * (1.0 + pre_gate * (1.0 - sigmoid_gate)))


def local_grads(pre_gate, pre_up, grad_act):
    active, slope_gate = silu_parts(pre_gate)
    hidden = (active * pre_up).astype(jnp.bfloat16)
    grad_gate = (grad_act * pre_up * slope_gate).astype(jnp.bfloat16)
    grad_up = (grad_act * active).astype(jnp.bfloat16)
    return (hidden, grad_gate, grad_up)


def shards(tokens, out_grad, expert_ids, gate_probs, w_gate, w_up, w_down):
    tok_rows, slab_width = tokens.shape
    owners = lax.axis_size("expert")
    experts = owners * w_gate.shape[0]
    pick_ids = expert_ids.T.reshape(-1)
    onehot = (pick_ids[:, None] == jnp.arange(experts, dtype=jnp.int32)[None, :]).astype(
        jnp.bfloat16
    )
    picks = pick_ids.shape[0]
    order = jnp.arange(picks, dtype=jnp.int32)
    earlier = (order[None, :] < order[:, None]).astype(jnp.bfloat16)
    before = jnp.dot(earlier, onehot, preferred_element_type=jnp.float32)
    rank_in = jnp.sum(before * onehot.astype(jnp.float32), axis=1).astype(jnp.int32)
    slot_of = pick_ids * MOST + rank_in
    placing = (jnp.arange(experts * MOST, dtype=jnp.int32)[:, None] == slot_of[None, :]).astype(
        jnp.bfloat16
    )
    row_pick = jnp.concatenate([tokens, tokens], axis=0)
    grad_pick = jnp.concatenate([out_grad, out_grad], axis=0)
    scaled = (gate_probs.T.reshape(-1)[:, None] * grad_pick.astype(jnp.float32)).astype(
        jnp.bfloat16
    )
    both = jnp.concatenate([row_pick, scaled], axis=1)
    send = (
        jnp.dot(placing, both, preferred_element_type=jnp.float32)
        .astype(jnp.bfloat16)
        .reshape(experts, MOST, 2 * slab_width)
    )
    arrived = lax.all_to_all(send, "expert", split_axis=0, concat_axis=0, tiled=True)
    arrived_tokens = arrived[:, :, :slab_width]
    arrived_grads = arrived[:, :, slab_width:]
    flat_tokens = arrived_tokens.reshape(-1, slab_width)
    flat_grads = arrived_grads.reshape(-1, slab_width)
    gate_mat = w_gate[0]
    up_mat = w_up[0]
    down_mat = w_down[0]
    part_gate = jnp.dot(flat_tokens, gate_mat, preferred_element_type=jnp.float32)
    part_up = jnp.dot(flat_tokens, up_mat, preferred_element_type=jnp.float32)
    part_act = lax.dot_general(
        flat_grads, down_mat, contract_cols, preferred_element_type=jnp.float32
    )
    pre_gate, pre_up, grad_act = (
        lax.psum(part_gate.astype(jnp.bfloat16), "dp").astype(jnp.float32),
        lax.psum(part_up.astype(jnp.bfloat16), "dp").astype(jnp.float32),
        lax.psum(part_act.astype(jnp.bfloat16), "dp").astype(jnp.float32),
    )
    hidden, grad_gate, grad_up = local_grads(pre_gate, pre_up, grad_act)
    grad_gate, grad_up = lax.optimization_barrier((grad_gate, grad_up))
    slot_grad = lax.dot_general(
        grad_gate, gate_mat, contract_cols, preferred_element_type=jnp.float32
    )
    slot_grad = slot_grad + lax.dot_general(
        grad_up, up_mat, contract_cols, preferred_element_type=jnp.float32
    )
    gate_grads = lax.dot_general(
        flat_tokens, grad_gate, contract_rows, preferred_element_type=jnp.float32
    )[None]
    up_grads = lax.dot_general(
        flat_tokens, grad_up, contract_rows, preferred_element_type=jnp.float32
    )[None]
    down_grads = lax.dot_general(
        hidden, flat_grads, contract_rows, preferred_element_type=jnp.float32
    )[None]
    returned = lax.all_to_all(
        slot_grad.reshape(experts, MOST, slab_width).astype(jnp.bfloat16),
        "expert",
        split_axis=0,
        concat_axis=0,
        tiled=True,
    )
    flat_back = returned.reshape(experts * MOST, slab_width)
    per_pick = lax.dot_general(
        placing, flat_back, contract_rows, preferred_element_type=jnp.float32
    )
    token_grad = (per_pick[:tok_rows] + per_pick[tok_rows:]).astype(jnp.bfloat16)
    return (token_grad, gate_grads, up_grads, down_grads)


def solution(mesh):
    in_specs = (
        P("expert", "dp"),
        P("expert", "dp"),
        P("expert", None),
        P("expert", None),
        P("expert", "dp", None),
        P("expert", "dp", None),
        P("expert", None, "dp"),
    )
    out_specs = (
        P("expert", "dp"),
        P("expert", "dp", None),
        P("expert", "dp", None),
        P("expert", None, "dp"),
    )
    return jax.shard_map(shards, mesh=mesh, in_specs=in_specs, out_specs=out_specs, check_vma=False)
```

profile of v0, /device:TPU:32, one launch (start us, length us, event | category | flops | bytes accessed | tf_op | source)
XLA Modules:
  0.0 285.1 jit_solution(2284455037294095577)
XLA Ops:
  7.2 0.0 all-reduce.3.cloned.1.call-start
  7.2 0.8 copy.11
  8.0 0.3 fusion.17
  8.3 0.7 copy.12
  9.0 1.2 multiply_convert_fusion
  10.2 2.3 fusion.13
  12.5 61.8 %all_to_all.10 = bf16[32,32,1024]{2,1,0:T(8,128)(2,1)S(1)} all-to-all(bf16[32,32,1024]{2,1,0:T(8,128)(2,1)S(1)} %bitcast.45), channel_id=1, replica_groups=mesh['dp'=8,'expert'=32] {'expert'}, dimensions={0} | all-to-all | bytes 4194304 | tf_op jit(solution)/shard_map/all_to_all | solution.py:52
  74.2 0.2 fusion.36
  74.5 2.6 convolution_convert_fusion
  77.1 2.6 convolution_convert_fusion.1
  79.6 2.6 convolution_convert_fusion.2
  82.3 146.2 %all-reduce.3.cloned.1.call-done = (bf16[1024,1024]{1,0:T(8,128)(2,1)}, bf16[1024,1024]{1,0:T(8,128)(2,1)}, bf16[1024,1024]{1,0:T(8,128)(2,1)}) async-done(((bf16[1024,1024]{1,0:T(8,128)(2,1)}, bf16[1024,1024]{1,0:T(8,128)(2,1)}, bf16[1024,1024]{1,0:T(8,128)(2,1)}), (bf16[1024,1024]{1,0:T(8,128)(2,1)}, bf16[1024,1024]{1,0:T(8,128)(2,1)}, bf16[1024,1024]{1,0:T(8,128)(2,1)})) %all-reduce.3.cloned.1.call-update) | async-done | bytes 6291472 | tf_op jit(solution)/shard_map/psum | solution.py:67
  228.5 4.2 %fusion = (bf16[1024,1024]{1,0:T(8,128)(2,1)S(1)}, bf16[1024,1024]{1,0:T(8,128)(2,1)S(1)}) fusion(bf16[1024,1024]{1,0:T(8,128)(2,1)} %get-tuple-element.9, bf16[1024,1024]{1,0:T(8,128)(2,1)} %get-tuple-element.10, bf16[1024,1024]{1,0:T(8,128)(2,1)} %get-tuple-element.8), kind=kLoop, calls=%fused_computation.6 | loop fusion | flops 16777216 | bytes 10485760 | tf_op jit(solution)/shard_map/convert_element_type | solution.py:20
  232.8 1.3 fusion.23
  234.1 0.7 copy-done.3
  234.8 2.2 add_convert_fusion
  237.0 10.0 %all-to-all-start.1 = ((bf16[32,32,512]{2,1,0:T(8,128)(2,1)}), bf16[32,32,512]{2,1,0:T(8,128)(2,1)S(1)}, u32[]{:S(2)}, u32[]{:S(2)}) async-start(bf16[32,32,512]{2,1,0:T(8,128)(2,1)} %bitcast.47), calls=%async_computation.1 | async-start | bytes 2097152 | tf_op jit(solution)/shard_map/all_to_all | solution.py:87
  247.1 4.3 %convolution_bitcast_fusion.1 = f32[1,512,1024]{2,1,0:T(8,128)} fusion(bf16[1024,512]{1,0:T(8,128)(2,1)S(1)} %bitcast.43, bf16[1024,1024]{1,0:T(8,128)(2,1)} %copy-done.3), kind=kOutput, calls=%fused_computation.26 | convolution fusion | flops 1073741824 | bytes 5242880 | tf_op jit(solution)/shard_map/dot_general | solution.py:78
  251.4 2.6 convolution_bitcast_fusion
  254.0 0.6 copy-done.7
  254.6 2.8 fusion.14
  257.4 19.3 %all-to-all-done.1 = bf16[32,32,512]{2,1,0:T(8,128)(2,1)S(1)} async-done(((bf16[32,32,512]{2,1,0:T(8,128)(2,1)}), bf16[32,32,512]{2,1,0:T(8,128)(2,1)S(1)}, u32[]{:S(2)}, u32[]{:S(2)}) %all-to-all-start.1) | async-done | bytes 1048608 | tf_op jit(solution)/shard_map/all_to_all | solution.py:87
  276.7 0.8 fusion.11
  277.5 0.8 fusion.31
  (20 shorter events, 0.1 us)
Async XLA Ops:
  7.2 67.3 %copy-start = (bf16[1,512,1024]{2,1,0:T(8,128)(2,1)S(1)}, bf16[1,512,1024]{2,1,0:T(8,128)(2,1)}, u32[]{:S(2)}) copy-start(bf16[1,512,1024]{2,1,0:T(8,128)(2,1)} %param.11) | copy-start | bytes 3145732
  7.2 221.3 %all-reduce.3.cloned.1.call-start = ((), (), s32[]{:S(2)}) async-start(), calls=%async_computation.2 | async-start | bytes 12582912 | tf_op jit(solution)/shard_map/psum | solution.py:67
  74.4 5.2 %copy-start.6 = (bf16[32,32,512]{2,1,0:T(8,128)(2,1)}, bf16[32,32,512]{2,1,0:T(8,128)(2,1)S(1)}, u32[]{:S(2)}) copy-start(bf16[32,32,512]{2,1,0:T(8,128)(2,1)S(1)} %get-tuple-element.13) | copy-start | bytes 3145732
  74.5 2.6 copy-start.9
  77.1 2.6 copy-start.8
  232.8 1.3 copy-start.1
  232.8 2.0 copy-start.3
  237.0 39.7 %all-to-all-start.1 = ((bf16[32,32,512]{2,1,0:T(8,128)(2,1)}), bf16[32,32,512]{2,1,0:T(8,128)(2,1)S(1)}, u32[]{:S(2)}, u32[]{:S(2)}) async-start(bf16[32,32,512]{2,1,0:T(8,128)(2,1)} %bitcast.47), calls=%async_computation.1 | async-start | bytes 2097152 | tf_op jit(solution)/shard_map/all_to_all | solution.py:87
  247.1 4.3 %copy-start.2 = (bf16[1024,1024]{1,0:T(8,128)(2,1)S(1)}, bf16[1024,1024]{1,0:T(8,128)(2,1)}, u32[]{:S(2)}) copy-start(bf16[1024,1024]{1,0:T(8,128)(2,1)} %copy-done.1) | copy-start | bytes 6291460
  251.4 2.6 copy-start.4
  251.4 2.6 copy-start.5
  251.4 3.2 %copy-start.7 = (bf16[32,32,512]{2,1,0:T(8,128)(2,1)S(1)}, bf16[32,32,512]{2,1,0:T(8,128)(2,1)}, u32[]{:S(2)}) copy-start(bf16[32,32,512]{2,1,0:T(8,128)(2,1)} %copy-done.6) | copy-start | bytes 3145732
Sparse Core Ops, SparseCore 0:
  82.4 146.0 all-reduce.2
where the time goes:
time: 285 us
  waiting for transfers between devices  166 us (58%)
  blocking collectives  61.8 us (22%)
  matrix products  24.3 us (9%)
  between operations  14.2 us (5%)
  starting transfers between devices  10.1 us (4%)
  other arithmetic  6.21 us (2%)
  local copies, waits for them, and re-layouts  2.97 us (1%)
    psum x1, waiting for transfers between devices, shards(): lax.psum(part_up.astype(jnp.bfloat16), 'dp').astype(jnp.float32)  146 us
    all_to_all x1, blocking collectives, shards(): lax.all_to_all(send, 'expert', split_axis=0, concat_axis=0, tiled=True)  61.8 us
    all_to_all x1, waiting for transfers between devices, shards(): lax.all_to_all(slot_grad.reshape(experts, MOST, slab_width).astype(jnp.bf...  19.3 us
    all_to_all x1, starting transfers between devices, shards(): lax.all_to_all(slot_grad.reshape(experts, MOST, slab_width).astype(jnp.bf...  10 us
  transfers between devices with their start and end apart: 2, of which 2 were waited for; matrix products, arithmetic and copies ran while one was open for 3% of the time, Pallas kernels for 0%

commit v1 on v0

--- a/solution.py
+++ b/solution.py
@@ -1,3 +1,4 @@
+import functools
 import jax
 import jax.numpy as jnp
 from jax import lax
@@ -6,6 +7,14 @@
 MOST = 32
 contract_rows = (((0,), (0,)), ((), ()))
 contract_cols = (((1,), (1,)), ((), ()))
+
+
+def arrange_threads(a0, net_axis):
+    u1 = jax.lax.all_gather(a0, net_axis).sum(axis=0)
+    return u1
+
+
+link_pieces_all_for = functools.partial(arrange_threads, net_axis="dp")
 
 
 def silu_parts(pre_gate):
@@ -64,7 +73,7 @@
     )
     pre_gate, pre_up, grad_act = (
         lax.psum(part_gate.astype(jnp.bfloat16), "dp").astype(jnp.float32),
-        lax.psum(part_up.astype(jnp.bfloat16), "dp").astype(jnp.float32),
+        link_pieces_all_for(part_up.astype(jnp.bfloat16)).astype(jnp.float32),
         lax.psum(part_act.astype(jnp.bfloat16), "dp").astype(jnp.float32),
     )
     hidden, grad_gate, grad_up = local_grads(pre_gate, pre_up, grad_act)

time: 285 us -> 417 us (1.46)
  waiting for transfers between devices: 166 us -> 285 us
  other arithmetic: 6.21 us -> 17 us
    all_gather x0 -> x1, waiting for transfers between devices: none -> 164 us  [arrange_threads(): u1 = jax.lax.all_gather(a0, net_axis).sum(axis=0)]
    psum x1, waiting for transfers between devices: 146 us -> 102 us  [shards(): lax.psum(part_act.astype(jnp.bfloat16), 'dp').astype(jnp.float32)]
    reduce_sum x0 -> x1, other arithmetic: none -> 10.8 us  [arrange_threads(): u1 = jax.lax.all_gather(a0, net_axis).sum(axis=0)]
  transfers between devices with their start and end apart: 2 -> 3, of which waited for: 2 -> 3; matrix products, arithmetic and copies ran while one was open for 3% -> 6% of each run, Pallas kernels for 0% -> 0%
where the time goes in v1:
time: 417 us
  waiting for transfers between devices  285 us (68%)
  blocking collectives  61.8 us (15%)
  matrix products  24.4 us (6%)
  other arithmetic  17 us (4%)
  between operations  14.2 us (3%)
  starting transfers between devices  10.1 us (2%)
    all_gather x1, waiting for transfers between devices, arrange_threads(): u1 = jax.lax.all_gather(a0, net_axis).sum(axis=0)  164 us
    psum x1, waiting for transfers between devices, shards(): lax.psum(part_act.astype(jnp.bfloat16), 'dp').astype(jnp.float32)  102 us
    all_to_all x1, blocking collectives, shards(): lax.all_to_all(send, 'expert', split_axis=0, concat_axis=0, tiled=True)  61.8 us
    all_to_all x1, waiting for transfers between devices, shards(): lax.all_to_all(slot_grad.reshape(experts, MOST, slab_width).astype(jnp.bf...  19.3 us
    reduce_sum x1, other arithmetic, arrange_threads(): u1 = jax.lax.all_gather(a0, net_axis).sum(axis=0)  10.8 us
    all_to_all x1, starting transfers between devices, shards(): lax.all_to_all(slot_grad.reshape(experts, MOST, slab_width).astype(jnp.bf...  10 us
  transfers between devices with their start and end apart: 3, of which 3 were waited for; matrix products, arithmetic and copies ran while one was open for 6% of the time, Pallas kernels for 0%

profile of v1, /device:TPU:32, one launch (start us, length us, event | category | flops | bytes accessed | tf_op | source)
XLA Modules:
  0.0 416.6 jit_solution(15794422687783754138)
XLA Ops:
  7.2 0.8 copy.11
  8.3 0.7 copy.12
  9.0 1.2 multiply_convert_fusion
  10.2 2.3 fusion.13
  12.5 61.8 %all_to_all.10 = bf16[32,32,1024]{2,1,0:T(8,128)(2,1)S(1)} all-to-all(bf16[32,32,1024]{2,1,0:T(8,128)(2,1)S(1)} %bitcast.47), channel_id=1, replica_groups=mesh['dp'=8,'expert'=32] {'expert'}, dimensions={0} | all-to-all | bytes 4194304 | tf_op jit(solution)/shard_map/all_to_all | solution.py:61
  74.6 0.9 copy-done.9
  75.5 2.6 convolution_convert_fusion.1
  78.1 2.6 convolution_convert_fusion
  80.7 2.6 convolution_convert_fusion.2
  83.3 164.1 %all-gather.3.cloned.1.call-done = bf16[8192,1024]{1,0:T(8,128)(2,1)} async-done(((bf16[1024,1024]{1,0:T(8,128)(2,1)}), bf16[8192,1024]{1,0:T(8,128)(2,1)}) %all-gather.3.cloned.1.call-update) | async-done | bytes 16777232 | tf_op jit(solution)/shard_map/all_gather | solution.py:13
  247.4 10.8 %reduce_sum.22 = bf16[1024,1024]{1,0:T(8,128)(2,1)} reduce(bf16[8,1024,1024]{2,1,0:T(8,128)(2,1)} %bitcast.42, bf16[]{:T(256)} %constant.6.clone.1), dimensions={0}, to_apply=%region_2.0 | reduce | flops 7340032 | bytes 18874370 | tf_op jit(solution)/shard_map/reduce_sum | solution.py:13
  258.2 101.7 %all-reduce.3.cloned.1.call-done = (bf16[1024,1024]{1,0:T(8,128)(2,1)}, bf16[1024,1024]{1,0:T(8,128)(2,1)}) async-done(((bf16[1024,1024]{1,0:T(8,128)(2,1)}, bf16[1024,1024]{1,0:T(8,128)(2,1)}), (bf16[1024,1024]{1,0:T(8,128)(2,1)}, bf16[1024,1024]{1,0:T(8,128)(2,1)})) %all-reduce.3.cloned.1.call-update) | async-done | bytes 4194320 | tf_op jit(solution)/shard_map/psum | solution.py:77
  360.0 4.2 %fusion = (bf16[1024,1024]{1,0:T(8,128)(2,1)S(1)}, bf16[1024,1024]{1,0:T(8,128)(2,1)S(1)}) fusion(bf16[1024,1024]{1,0:T(8,128)(2,1)} %get-tuple-element.8, bf16[1024,1024]{1,0:T(8,128)(2,1)} %get-tuple-element.9, bf16[1024,1024]{1,0:T(8,128)(2,1)} %reduce_sum.22), kind=kLoop, calls=%fused_computation.6 | loop fusion | flops 16777216 | bytes 10485760 | tf_op jit(solution)/shard_map/convert_element_type | solution.py:29
  364.2 1.3 fusion.23
  365.5 0.7 copy-done.3
  366.3 2.3 add_convert_fusion
  368.5 10.0 %all-to-all-start.1 = ((bf16[32,32,512]{2,1,0:T(8,128)(2,1)}), bf16[32,32,512]{2,1,0:T(8,128)(2,1)S(1)}, u32[]{:S(2)}, u32[]{:S(2)}) async-start(bf16[32,32,512]{2,1,0:T(8,128)(2,1)} %bitcast.49), calls=%async_computation.1 | async-start | bytes 2097152 | tf_op jit(solution)/shard_map/all_to_all | solution.py:96
  378.6 4.3 %convolution_bitcast_fusion.1 = f32[1,512,1024]{2,1,0:T(8,128)} fusion(bf16[1024,512]{1,0:T(8,128)(2,1)S(1)} %bitcast.45, bf16[1024,1024]{1,0:T(8,128)(2,1)} %copy-done.3), kind=kOutput, calls=%fused_computation.26 | convolution fusion | flops 1073741824 | bytes 5242880 | tf_op jit(solution)/shard_map/dot_general | solution.py:87
  382.9 2.6 convolution_bitcast_fusion
  385.5 0.6 copy-done.7
  386.1 2.8 fusion.14
  388.9 19.3 %all-to-all-done.1 = bf16[32,32,512]{2,1,0:T(8,128)(2,1)S(1)} async-done(((bf16[32,32,512]{2,1,0:T(8,128)(2,1)}), bf16[32,32,512]{2,1,0:T(8,128)(2,1)S(1)}, u32[]{:S(2)}, u32[]{:S(2)}) %all-to-all-start.1) | async-done | bytes 1048608 | tf_op jit(solution)/shard_map/all_to_all | solution.py:96
  408.2 0.8 fusion.11
  409.0 0.8 fusion.31
  (26 shorter events, 0.8 us)
Async XLA Ops:
  7.2 71.0 %copy-start = (bf16[1,512,1024]{2,1,0:T(8,128)(2,1)S(1)}, bf16[1,512,1024]{2,1,0:T(8,128)(2,1)}, u32[]{:S(2)}) copy-start(bf16[1,512,1024]{2,1,0:T(8,128)(2,1)} %param.11) | copy-start | bytes 3145732
  7.2 240.2 %all-gather.3.cloned.1.call-start = ((), (), s32[]{:S(2)}) async-start(), calls=%async_computation.2 | async-start | bytes 18874368 | tf_op jit(solution)/shard_map/all_gather | solution.py:13
  74.2 1.2 copy-start.9
  74.5 6.2 %copy-start.6 = (bf16[32,32,512]{2,1,0:T(8,128)(2,1)}, bf16[32,32,512]{2,1,0:T(8,128)(2,1)S(1)}, u32[]{:S(2)}) copy-start(bf16[32,32,512]{2,1,0:T(8,128)(2,1)S(1)} %get-tuple-element.12) | copy-start | bytes 3145732
  78.1 281.9 %all-reduce.3.cloned.1.call-start = ((), (), s32[]{:S(2)}) async-start(), calls=%async_computation.3 | async-start | bytes 8388608 | tf_op jit(solution)/shard_map/psum | solution.py:77
  78.1 2.6 copy-start.8
  364.2 1.3 copy-start.1
  364.2 2.0 copy-start.3
  364.2 2.0 copy-start.10
  368.5 39.7 %all-to-all-start.1 = ((bf16[32,32,512]{2,1,0:T(8,128)(2,1)}), bf16[32,32,512]{2,1,0:T(8,128)(2,1)S(1)}, u32[]{:S(2)}, u32[]{:S(2)}) async-start(bf16[32,32,512]{2,1,0:T(8,128)(2,1)} %bitcast.49), calls=%async_computation.1 | async-start | bytes 2097152 | tf_op jit(solution)/shard_map/all_to_all | solution.py:96
  378.6 4.3 %copy-start.2 = (bf16[1024,1024]{1,0:T(8,128)(2,1)S(1)}, bf16[1024,1024]{1,0:T(8,128)(2,1)}, u32[]{:S(2)}) copy-start(bf16[1024,1024]{1,0:T(8,128)(2,1)} %copy-done.1) | copy-start | bytes 6291460
  382.9 2.6 copy-start.4
  382.9 2.6 copy-start.5
  382.9 3.2 copy-start.7
Sparse Core Ops, SparseCore 0:
  78.2 169.1 all-gather.2
  250.7 109.2 all-reduce.2
